TPU v7x, 32 devices: a whole 2x2x4 slice. The times are simulated.
32 devices in a mesh: beam: 2 (over y), band: 16 (over z, x, core).
Axes of the slice: x: 2, y: 2, z: 4, core: 2. Of those that a mesh axis runs over, the one named last changes fastest.
Arguments:
- filterbank: float32 [1024, 6144], P(('beam', 'band')), parts along dimension 0, may hold values from -40 to 40
- offsets: int32 [9, 512], P(None, 'band'), may hold values from 0 to 255, as said below
- widths: int32 [8], replicated, may hold values from 1 to 128, as said below
Outputs:
- detection: float32 [1024, 2048], P(('beam', 'band')), parts along dimension 0
- peak_series: float32 [4096], P('beam'), parts along dimension 0
There are 2 independent parts, one for each index of `beam`. A program takes and returns all parts, laid end to end along the dimension named above; an argument that names none is the same for every part. Nothing has to cross between parts.
Inputs may be any that keep to these rules, and one draw needn't show every extreme that they name: `offsets`: in every section some offset equals 255. Among the 8 widths are 1 and 128.
All inputs are finite; a program needn't handle non-finite values.
Results may differ from a plain program's by a relative error of at most 0.0002.
Values sent between devices are 32-bit elements; how exact they have to be, the bound alone decides.
No kernel may reach another device: no remote copies, remote signals or barrier semaphores. Data moves between devices by JAX's collectives and lax.ppermute only.
A program may use at most 64 MiB of HBM per device.

v0:
```python
import math
import jax
import jax.numpy as jnp
from jax import lax
from jax.sharding import PartitionSpec as P

TS = 2048
TIN = 6144
SHIFT = 256
TAPS = 128
TEMPLATES = 8


def from_partner(value, axis, distance):
    mask = 2**distance
    pairs = [(source, source ^ mask) for source in range(lax.axis_size(axis))]
    return lax.ppermute(value, axis, pairs)


def shift_rows(trial_rows, amounts, length):
    current = jnp.pad(trial_rows, ((0, 0), (0, 2 * SHIFT)))
    top_bit = (SHIFT - 1).bit_length()
    for bit_index in reversed(range(top_bit)):
        span = 2**bit_index
        keep_len = length + span - 1
        chosen = (amounts >> bit_index & 1)[:, None] == 1
        current = jnp.where(chosen, current[:, span : span + keep_len], current[:, :keep_len])
    return current


def merge_section(current, offsets_now, section_index, new_length):
    group_trials = 2**section_index
    total_rows = current.shape[0]
    groups = total_rows // (2 * group_trials)
    blocks = current.reshape(groups, 2, group_trials, current.shape[1])
    lower_part = blocks[:, 0, :, :new_length]
    upper_flat = blocks[:, 1].reshape(groups * group_trials, current.shape[1])
    amounts = offsets_now.reshape(groups, 2, group_trials)
    first_half = lower_part + shift_rows(upper_flat, amounts[:, 0].reshape(-1), new_length).reshape(
        groups, group_trials, new_length
    )
    second_half = lower_part + shift_rows(
        upper_flat, amounts[:, 1].reshape(-1), new_length
    ).reshape(groups, group_trials, new_length)
    return jnp.stack([first_half, second_half], axis=1).reshape(total_rows, new_length)


def template_tables(widths):
    source = lax.broadcasted_iota(jnp.int32, (2 * TAPS, TAPS), 0)
    target = lax.broadcasted_iota(jnp.int32, (2 * TAPS, TAPS), 1)
    tap_offset = source - target
    inside = (tap_offset[None] >= 0) & (tap_offset[None] < widths[:, None, None])
    tap_scale = 1.0 / jnp.sqrt(widths.astype(jnp.float32))
    return jnp.where(inside, tap_scale[:, None, None], jnp.zeros((), jnp.float32))


def boxcar_max(dedispersed, widths):
    total_rows = dedispersed.shape[0]
    blocks_time = TS // TAPS
    window = dedispersed.reshape(total_rows, blocks_time + 1, TAPS)
    paired = jnp.concatenate([window[:, :-1], window[:, 1:]], axis=2).reshape(
        total_rows * blocks_time, 2 * TAPS
    )
    tables = template_tables(widths)
    best_value = None
    for template_index in range(TEMPLATES):
        result = jnp.dot(
            paired,
            tables[template_index],
            precision=lax.Precision.HIGHEST,
            preferred_element_type=jnp.float32,
        )
        if template_index == 0:
            best_value = result
        else:
            best_value = jnp.maximum(best_value, result)
    return best_value.reshape(total_rows, TS)


def per_device(filterbank, offsets, widths):
    levels = offsets.shape[0]
    local_count = filterbank.shape[0].bit_length() - 1
    band_count = lax.axis_size("band")
    channels_all = filterbank.shape[0] * band_count

    def length_after(sections_done):
        needed = TS + TAPS + (levels - sections_done) * (SHIFT - 1)
        needed = -(-needed // 128) * 128
        return min(TIN, needed)

    partial_value = jnp.sum(filterbank, axis=0)
    channel_mean = lax.psum(partial_value, "band") / channels_all
    current = filterbank - channel_mean[None, :]
    for local_section_index in range(local_count):
        current = merge_section(
            current,
            offsets[local_section_index],
            local_section_index,
            length_after(local_section_index + 1),
        )
    band_index = lax.axis_index("band")
    for bit_index in range(band_count.bit_length() - 1):
        section_index = local_count + bit_index
        new_length = length_after(section_index + 1)
        partner = from_partner(current, "band", bit_index)
        upper_half = band_index // 2**bit_index % 2 == 1
        lower_part = jnp.where(upper_half, partner, current)
        upper_part = jnp.where(upper_half, current, partner)
        current = lower_part[:, :new_length] + shift_rows(
            upper_part, offsets[section_index], new_length
        )
    dedispersed = current * (1.0 / math.sqrt(channels_all))
    detection = boxcar_max(dedispersed, widths)
    peak_series = lax.pmax(jnp.max(detection, axis=0), "band")
    return (detection, peak_series)


def solution(mesh):
    placed = (P(("beam", "band"), None), P(None, "band"), P())
    return jax.shard_map(
        per_device,
        mesh=mesh,
        in_specs=placed,
        out_specs=(P(("beam", "band"), None), P("beam")),
        check_vma=False,
    )
```

profile of v0, /device:TPU:0, one launch (start us, length us, event | category | flops | bytes accessed | tf_op | source)
XLA Modules:
  0.0 164.7 jit_solution(757025383159185364)
XLA Ops:
  0.6 1.3 reduce_sum.9
  1.9 62.9 %psum.7 = f32[6144]{0:T(1024)S(1)} all-reduce(f32[6144]{0:T(1024)S(1)} %reduce_sum.9), channel_id=1, replica_groups=mesh['beam'=2,'band'=16] {'band'}, use_global_device_ids=true, to_apply=%region_1.0 | all-reduce | flops 6144 | bytes 49152 | tf_op jit(solution)/shard_map/psum | solution.py:92
  64.9 0.5 reshape.1647
  65.4 0.2 slice.1056
  65.6 0.4 slice.1058
  66.0 0.3 copy-done.2
  69.7 0.4 fusion.24
  70.1 0.2 compare_reduce_fusion.15
  73.5 0.2 slice_select_fusion.36
  73.7 0.2 fusion.5
  74.3 0.3 slice.1092
  74.8 0.2 reshape_squeeze.43
  77.4 0.6 copy_add_fusion.1
  77.9 0.5 pad_maximum_fusion.1
  78.5 0.3 reshape_reshape.10
  78.8 0.3 slice.1126
  81.4 0.6 copy_add_fusion.3
  81.9 0.4 pad_maximum_fusion.2
  82.5 0.2 reshape_reshape.11
  83.6 0.3 slice_select_fusion.89
  84.6 0.2 fusion.10
  86.5 0.2 fusion.14
  86.8 1.7 %collective-permute-done = f32[32,3200]{1,0:T(8,128)S(1)} collective-permute-done((f32[32,3200]{1,0:T(8,128)S(1)}, f32[32,3200]{1,0:T(8,128)S(1)}, u32[]{:S(2)}, u32[]{:S(2)}) %collective-permute-start) | collective-permute-done | bytes 409632 | tf_op jit(solution)/shard_map/ppermute | solution.py:17
  88.6 0.2 slice_select_fusion.5
  88.8 0.2 slice_select_fusion.4
  89.0 0.2 slice_select_fusion.3
  89.2 0.2 slice_select_fusion.2
  89.3 0.2 slice_select_fusion.1
  89.5 0.2 slice_select_fusion
  89.7 0.2 fusion
  90.0 10.8 %collective-permute-done.1 = f32[32,2944]{1,0:T(8,128)S(1)} collective-permute-done((f32[32,2944]{1,0:T(8,128)S(1)}, f32[32,2944]{1,0:T(8,128)S(1)}, u32[]{:S(2)}, u32[]{:S(2)}) %collective-permute-start.1) | collective-permute-done | bytes 376864 | tf_op jit(solution)/shard_map/ppermute | solution.py:17
  101.2 0.2 slice_select_fusion.12
  101.4 0.2 slice_select_fusion.11
  101.9 0.2 fusion.1
  102.2 0.6 copy-done.3
  102.9 8.5 %collective-permute-done.2 = f32[32,2688]{1,0:T(8,128)S(1)} collective-permute-done((f32[32,2688]{1,0:T(8,128)S(1)}, f32[32,2688]{1,0:T(8,128)S(1)}, u32[]{:S(2)}, u32[]{:S(2)}) %collective-permute-start.2) | collective-permute-done | bytes 344096 | tf_op jit(solution)/shard_map/ppermute | solution.py:17
  112.5 0.2 fusion.2
  112.8 0.2 and_select_fusion
  113.0 14.9 %collective-permute-done.3 = f32[32,2432]{1,0:T(8,128)S(1)} collective-permute-done((f32[32,2432]{1,0:T(8,128)S(1)}, f32[32,2432]{1,0:T(8,128)S(1)}, u32[]{:S(2)}, u32[]{:S(2)}) %collective-permute-start.3) | collective-permute-done | bytes 311328 | tf_op jit(solution)/shard_map/ppermute | solution.py:17
  129.3 0.6 fusion.15
  129.9 0.6 convolution_maximum_fusion.6
  130.5 0.6 convolution_maximum_fusion.5
  131.0 0.6 convolution_maximum_fusion.4
  131.6 0.6 convolution_maximum_fusion.3
  132.2 0.6 convolution_maximum_fusion.2
  132.8 0.6 convolution_maximum_fusion.1
  133.4 0.6 convolution_maximum_fusion
  134.1 30.6 %pmax.7 = f32[2048]{0:T(1024)} all-reduce(f32[2048]{0:T(1024)S(1)} %reduce_max.9), channel_id=1, replica_groups=mesh['beam'=2,'band'=16] {'band'}, use_global_device_ids=true, to_apply=%region_3.4 | all-reduce | flops 2048 | bytes 16384 | tf_op jit(solution)/shard_map/pmax | solution.py:114
  (188 shorter events, 18.4 us)
Async XLA Ops:
  0.6 64.2 %copy-start = (f32[32,6144]{1,0:T(8,128)S(1)}, f32[32,6144]{1,0:T(8,128)}, u32[]{:S(2)}) copy-start(f32[32,6144]{1,0:T(8,128)} %param.3) | copy-start | bytes 2359300
  65.6 0.7 copy-start.2
  86.7 1.8 %collective-permute-start = (f32[32,3200]{1,0:T(8,128)S(1)}, f32[32,3200]{1,0:T(8,128)S(1)}, u32[]{:S(2)}, u32[]{:S(2)}) collective-permute-start(f32[32,3200]{1,0:T(8,128)S(1)} %bitcast.180), channel_id=1, source_target_pairs={{0,1},{1,0},{2,3},{3,2},{4,5},{5,4},{6,7},{7,6},{8,9},{9,8},{10,11... | collective-permute-start | bytes 1228808 | tf_op jit(solution)/shard_map/ppermute | solution.py:17
  89.9 10.9 %collective-permute-start.1 = (f32[32,2944]{1,0:T(8,128)S(1)}, f32[32,2944]{1,0:T(8,128)S(1)}, u32[]{:S(2)}, u32[]{:S(2)}) collective-permute-start(f32[32,2944]{1,0:T(8,128)S(1)} %fusion), channel_id=1, source_target_pairs={{0,2},{1,3},{2,0},{3,1},{4,6},{5,7},{6,4},{7,5},{8,10},{9,11},{10,... | collective-permute-start | bytes 1130504 | tf_op jit(solution)/shard_map/ppermute | solution.py:17
  102.1 9.3 %collective-permute-start.2 = (f32[32,2688]{1,0:T(8,128)S(1)}, f32[32,2688]{1,0:T(8,128)S(1)}, u32[]{:S(2)}, u32[]{:S(2)}) collective-permute-start(f32[32,2688]{1,0:T(8,128)S(1)} %fusion.1), channel_id=1, source_target_pairs={{0,4},{1,5},{2,6},{3,7},{4,0},{5,1},{6,2},{7,3},{8,12},{9,13},{10,... | collective-permute-start | bytes 1032200 | tf_op jit(solution)/shard_map/ppermute | solution.py:17
  102.2 0.7 copy-start.3
  112.7 15.3 %collective-permute-start.3 = (f32[32,2432]{1,0:T(8,128)S(1)}, f32[32,2432]{1,0:T(8,128)S(1)}, u32[]{:S(2)}, u32[]{:S(2)}) collective-permute-start(f32[32,2432]{1,0:T(8,128)S(1)} %fusion.2), channel_id=1, source_target_pairs={{0,8},{1,9},{2,10},{3,11},{4,12},{5,13},{6,14},{7,15},{8,0},{9,1},... | collective-permute-start | bytes 933896 | tf_op jit(solution)/shard_map/ppermute | solution.py:17
  134.0 30.6 %copy-start.1 = (f32[32,2048]{1,0:T(8,128)}, f32[32,2048]{1,0:T(8,128)S(1)}, u32[]{:S(2)}) copy-start(f32[32,2048]{1,0:T(8,128)S(1)} %reshape.1657) | copy-start | bytes 786436
where the time goes:
time: 165 us
  blocking collectives  93.5 us (57%)
  waiting for transfers between devices  35.9 us (22%)
  other arithmetic  19.1 us (12%)
  local copies, waits for them, and re-layouts  9.32 us (6%)
  matrix products  4.65 us (3%)
  between operations  1.91 us (1%)
    psum x1, blocking collectives, per_device(): channel_mean = lax.psum(partial_value, 'band') / channels_all  62.9 us
    ppermute x4, waiting for transfers between devices, from_partner(): return lax.ppermute(value, axis, pairs)  35.9 us
    pmax x1, blocking collectives, per_device(): peak_series = lax.pmax(jnp.max(detection, axis=0), 'band')  30.6 us
    select_n x96, other arithmetic, shift_rows(): jnp.where(chosen, current[:, span:span + keep_len], current[:, :keep_len])  13 us
    dot_general x8, matrix products, boxcar_max(): jnp.dot(paired, tables[template_index], precision=lax.Precision.HIGHEST,...  4.65 us
    eq x48, local copies, waits for them, and re-layouts, shift_rows(): chosen = (amounts >> bit_index & 1)[:, None] == 1  4.15 us
  transfers between devices with their start and end apart: 4, of which 4 were waited for; matrix products, arithmetic and copies ran while one was open for 0% of the time, Pallas kernels for 0%

commit v1 on v0

--- a/solution.py
+++ b/solution.py
@@ -9,6 +9,12 @@
 SHIFT = 256
 TAPS = 128
 TEMPLATES = 8
+
+
+def gather_and_add(block, axis):
+    pieces = lax.all_gather(block, axis, axis=0, tiled=False)
+    result = pieces.sum(axis=0)
+    return result
 
 
 def from_partner(value, axis, distance):
@@ -89,7 +95,7 @@
         return min(TIN, needed)
 
     partial_value = jnp.sum(filterbank, axis=0)
-    channel_mean = lax.psum(partial_value, "band") / channels_all
+    channel_mean = gather_and_add(partial_value, "band") / channels_all
     current = filterbank - channel_mean[None, :]
     for local_section_index in range(local_count):
         current = merge_section(

time: 165 us -> 127 us (0.77)
  blocking collectives: 93.5 us -> 54.8 us
    psum x1 -> x0, blocking collectives: 62.9 us -> none  [per_device(): channel_mean = lax.psum(partial_value, 'band') / channels_all]
    all_gather x0 -> x1, blocking collectives: none -> 24.3 us  [gather_and_add(): pieces = lax.all_gather(block, axis, axis=0, tiled=False)]
where the time goes in v1:
time: 127 us
  blocking collectives  54.8 us (43%)
  waiting for transfers between devices  36.3 us (29%)
  other arithmetic  19.1 us (15%)
  local copies, waits for them, and re-layouts  9.38 us (7%)
  matrix products  4.66 us (4%)
  between operations  1.91 us (2%)
    ppermute x4, waiting for transfers between devices, from_partner(): return lax.ppermute(value, axis, pairs)  36.3 us
    pmax x1, blocking collectives, per_device(): peak_series = lax.pmax(jnp.max(detection, axis=0), 'band')  30.6 us
    all_gather x1, blocking collectives, gather_and_add(): pieces = lax.all_gather(block, axis, axis=0, tiled=False)  24.3 us
    select_n x96, other arithmetic, shift_rows(): jnp.where(chosen, current[:, span:span + keep_len], current[:, :keep_len])  13 us
    dot_general x8, matrix products, boxcar_max(): jnp.dot(paired, tables[template_index], precision=lax.Precision.HIGHEST,...  4.66 us
    eq x48, local copies, waits for them, and re-layouts, shift_rows(): chosen = (amounts >> bit_index & 1)[:, None] == 1  4.15 us
  transfers between devices with their start and end apart: 4, of which 4 were waited for; matrix products, arithmetic and copies ran while one was open for 0% of the time, Pallas kernels for 0%

profile of v1, /device:TPU:0, one launch (start us, length us, event | category | flops | bytes accessed | tf_op | source)
XLA Modules:
  0.0 126.8 jit_solution(3325731299199960928)
XLA Ops:
  0.6 1.2 reduce_sum.18
  1.9 24.3 %all-gather = f32[98304]{0:T(1024)S(1)} all-gather(f32[6144]{0:T(1024)S(1)} %reduce_sum.18), channel_id=2, replica_groups=mesh['beam'=2,'band'=16] {'band'}, dimensions={0}, use_global_device_ids=true | all-gather | bytes 417792 | tf_op jit(solution)/shard_map/all_gather | solution.py:15
  26.4 0.5 reshape.1649
  26.8 0.2 slice.1056
  27.0 0.4 slice.1058
  27.4 0.3 copy-done.2
  31.1 0.4 fusion.24
  31.6 0.2 compare_reduce_fusion.15
  34.9 0.2 slice_select_fusion.36
  35.2 0.2 fusion.5
  35.8 0.3 slice.1092
  36.2 0.2 reshape_squeeze.43
  38.8 0.6 copy_add_fusion.1
  39.4 0.5 pad_maximum_fusion.1
  39.9 0.3 reshape_reshape.10
  40.2 0.3 slice.1126
  42.8 0.6 copy_add_fusion.3
  43.4 0.4 pad_maximum_fusion.2
  43.9 0.2 reshape_reshape.11
  44.5 0.3 slice_select_fusion.93
  46.0 0.2 fusion.10
  47.9 0.2 fusion.14
  48.1 0.4 collective-permute-start
  48.6 1.3 %collective-permute-done = f32[32,3200]{1,0:T(8,128)S(1)} collective-permute-done((f32[32,3200]{1,0:T(8,128)S(1)}, f32[32,3200]{1,0:T(8,128)S(1)}, u32[]{:S(2)}, u32[]{:S(2)}) %collective-permute-start) | collective-permute-done | bytes 409632 | tf_op jit(solution)/shard_map/ppermute | solution.py:23
  50.1 0.2 slice_select_fusion.5
  50.2 0.2 slice_select_fusion.4
  50.4 0.2 slice_select_fusion.3
  50.6 0.2 slice_select_fusion.2
  50.8 0.2 slice_select_fusion.1
  50.9 0.2 slice_select_fusion
  51.1 0.2 fusion
  51.4 11.0 %collective-permute-done.1 = f32[32,2944]{1,0:T(8,128)S(1)} collective-permute-done((f32[32,2944]{1,0:T(8,128)S(1)}, f32[32,2944]{1,0:T(8,128)S(1)}, u32[]{:S(2)}, u32[]{:S(2)}) %collective-permute-start.1) | collective-permute-done | bytes 376864 | tf_op jit(solution)/shard_map/ppermute | solution.py:23
  62.9 0.2 slice_select_fusion.12
  63.5 0.2 fusion.1
  63.9 0.6 copy-done.3
  64.5 8.8 %collective-permute-done.2 = f32[32,2688]{1,0:T(8,128)S(1)} collective-permute-done((f32[32,2688]{1,0:T(8,128)S(1)}, f32[32,2688]{1,0:T(8,128)S(1)}, u32[]{:S(2)}, u32[]{:S(2)}) %collective-permute-start.2) | collective-permute-done | bytes 344096 | tf_op jit(solution)/shard_map/ppermute | solution.py:23
  74.4 0.2 fusion.2
  74.6 0.2 and_select_fusion
  74.9 15.2 %collective-permute-done.3 = f32[32,2432]{1,0:T(8,128)S(1)} collective-permute-done((f32[32,2432]{1,0:T(8,128)S(1)}, f32[32,2432]{1,0:T(8,128)S(1)}, u32[]{:S(2)}, u32[]{:S(2)}) %collective-permute-start.3) | collective-permute-done | bytes 311328 | tf_op jit(solution)/shard_map/ppermute | solution.py:23
  91.4 0.6 fusion.15
  92.0 0.6 convolution_maximum_fusion.6
  92.6 0.6 convolution_maximum_fusion.5
  93.2 0.6 convolution_maximum_fusion.4
  93.8 0.6 convolution_maximum_fusion.3
  94.3 0.6 convolution_maximum_fusion.2
  94.9 0.6 convolution_maximum_fusion.1
  95.5 0.6 convolution_maximum_fusion
  96.2 30.6 %pmax.7 = f32[2048]{0:T(1024)} all-reduce(f32[2048]{0:T(1024)S(1)} %reduce_max.9), channel_id=1, replica_groups=mesh['beam'=2,'band'=16] {'band'}, use_global_device_ids=true, to_apply=%region_3.4 | all-reduce | flops 2048 | bytes 16384 | tf_op jit(solution)/shard_map/pmax | solution.py:120
  (190 shorter events, 18.6 us)
Async XLA Ops:
  1.8 24.4 %copy-start = (f32[32,6144]{1,0:T(8,128)S(1)}, f32[32,6144]{1,0:T(8,128)}, u32[]{:S(2)}) copy-start(f32[32,6144]{1,0:T(8,128)} %param.3) | copy-start | bytes 2359300
  27.0 0.7 copy-start.2
  48.1 1.8 %collective-permute-start = (f32[32,3200]{1,0:T(8,128)S(1)}, f32[32,3200]{1,0:T(8,128)S(1)}, u32[]{:S(2)}, u32[]{:S(2)}) collective-permute-start(f32[32,3200]{1,0:T(8,128)S(1)} %bitcast.180), channel_id=1, source_target_pairs={{0,1},{1,0},{2,3},{3,2},{4,5},{5,4},{6,7},{7,6},{8,9},{9,8},{10,11... | collective-permute-start | bytes 1228808 | tf_op jit(solution)/shard_map/ppermute | solution.py:23
  51.3 11.1 %collective-permute-start.1 = (f32[32,2944]{1,0:T(8,128)S(1)}, f32[32,2944]{1,0:T(8,128)S(1)}, u32[]{:S(2)}, u32[]{:S(2)}) collective-permute-start(f32[32,2944]{1,0:T(8,128)S(1)} %fusion), channel_id=1, source_target_pairs={{0,2},{1,3},{2,0},{3,1},{4,6},{5,7},{6,4},{7,5},{8,10},{9,11},{10,... | collective-permute-start | bytes 1130504 | tf_op jit(solution)/shard_map/ppermute | solution.py:23
  63.7 9.6 %collective-permute-start.2 = (f32[32,2688]{1,0:T(8,128)S(1)}, f32[32,2688]{1,0:T(8,128)S(1)}, u32[]{:S(2)}, u32[]{:S(2)}) collective-permute-start(f32[32,2688]{1,0:T(8,128)S(1)} %fusion.1), channel_id=1, source_target_pairs={{0,4},{1,5},{2,6},{3,7},{4,0},{5,1},{6,2},{7,3},{8,12},{9,13},{10,... | collective-permute-start | bytes 1032200 | tf_op jit(solution)/shard_map/ppermute | solution.py:23
  63.8 0.7 copy-start.3
  74.5 15.5 %collective-permute-start.3 = (f32[32,2432]{1,0:T(8,128)S(1)}, f32[32,2432]{1,0:T(8,128)S(1)}, u32[]{:S(2)}, u32[]{:S(2)}) collective-permute-start(f32[32,2432]{1,0:T(8,128)S(1)} %fusion.2), channel_id=1, source_target_pairs={{0,8},{1,9},{2,10},{3,11},{4,12},{5,13},{6,14},{7,15},{8,0},{9,1},... | collective-permute-start | bytes 933896 | tf_op jit(solution)/shard_map/ppermute | solution.py:23
  96.2 30.6 %copy-start.1 = (f32[32,2048]{1,0:T(8,128)}, f32[32,2048]{1,0:T(8,128)S(1)}, u32[]{:S(2)}) copy-start(f32[32,2048]{1,0:T(8,128)S(1)} %reshape.1659) | copy-start | bytes 786436
